TPU v7x, 256 devices: a whole 4x4x8 slice. The times are simulated.
256 devices in a mesh: row: 8 (over y, core), col: 8 (over z_hi, x), page: 4 (over z_lo).
Axes of the slice: x: 4, y: 4, z: 8 (z_hi: 2, z_lo: 4; z = z_hi * 4 + z_lo), core: 2. Of those that a mesh axis runs over, the one named last changes fastest.
Arguments:
- tokens: bfloat16 [32, 512, 2048], P(('row', 'page'), None, 'col'), may hold values from -6 to 6
- lengths: int32 [32], P(('row', 'page')), may hold values from 1 to 512, 4096 in all
- page_slot: int32 [32, 4], P('row'), may hold values from 0 to 15, as said below
- w_query: float32 [2048, 1024], P(('row', 'page'), 'col'), may hold values from -0.125 to 0.125
- w_keyval: float32 [2, 2048, 256], P(None, ('row', 'page')), may hold values from -0.125 to 0.125
- w_out: float32 [1024, 2048], P('col', ('row', 'page')), may hold values from -0.1875 to 0.1875
- w_gateup: float32 [2, 2048, 5120], P(None, ('row', 'page'), 'col'), may hold values from -0.125 to 0.125
- w_down: float32 [5120, 2048], P('col', ('row', 'page')), may hold values from -0.078125 to 0.078125
- attn_gain: float32 [2048], replicated, may hold values from 0.1 to 1.9
- ffn_gain: float32 [2048], replicated, may hold values from 0.1 to 1.9
- query_gain: float32 [64], replicated, may hold values from 0.1 to 1.9
- key_gain: float32 [64], replicated, may hold values from 0.1 to 1.9
Outputs:
- layer_out: bfloat16 [32, 512, 2048], P(('row', 'page'), None, 'col')
- kv_pages: bfloat16 [2, 128, 128, 1024], P(None, ('row', 'page'), None, 'col')
Inputs may be any that keep to these rules, and one draw needn't show every extreme that they name: `lengths`: each prompt's real tokens; in every draw some prompt has exactly 512. `page_slot`: within the prompts of one index of row the values are a permutation; page v belongs to index v // 4 of page; the 4 blocks of the prompts of one device send the same number of blocks to each of the 4 indices of page.
All inputs are finite; a program needn't handle non-finite values. No bound on the sum of `lengths` on one device may be relied on, other than what follows from the above.
Results may differ from a plain program's by a relative error of at most 0.012.
Values may be sent and summed in bfloat16 or wider, within the bound.
No kernel may reach another device: no remote copies, remote signals or barrier semaphores. Data moves between devices by JAX's collectives and lax.ppermute only.
A program may use at most 64 MiB of HBM per device.

v0:
```python
import jax
import jax.numpy as jnp
from jax import lax
from jax.sharding import PartitionSpec as P

PAGE_LEN = 128


def normalize(values, norm_gain):
    mean_sq = jnp.mean(values * values, axis=-1, keepdims=True)
    return values * lax.rsqrt(mean_sq + 1e-06) * norm_gain


def rotate(values):
    row_count = values.shape[-3]
    head_dim = values.shape[-1]
    half_dim = head_dim // 2
    frequency = 10000.0 ** (-2.0 * jnp.arange(half_dim, dtype=jnp.float32) / head_dim)
    angles = jnp.arange(row_count, dtype=jnp.float32)[:, None] * frequency[None, :]
    cosine = jnp.cos(angles)[:, None, :]
    sine_table = jnp.sin(angles)[:, None, :]
    leading = values[..., :half_dim]
    trailing = values[..., half_dim:]
    return jnp.concatenate(
        [leading * cosine - trailing * sine_table, trailing * cosine + leading * sine_table],
        axis=-1,
    )


def attend(query_rows, key_rows, value_rows, length):
    row_count = query_rows.shape[0]
    scores = jnp.einsum(
        "qhd,khd->hqk", query_rows, key_rows, preferred_element_type=jnp.float32
    ) * query_rows.shape[2] ** (-0.5)
    positions = jnp.arange(row_count, dtype=jnp.int32)
    seen_keys = (positions[None, :] <= positions[:, None]) & (positions[None, :] < length)
    exp_scores = jnp.where(seen_keys[None], jnp.exp(scores), 0.0)
    attn_probs = (exp_scores / jnp.sum(exp_scores, axis=-1, keepdims=True)).astype(jnp.bfloat16)
    attended = jnp.einsum(
        "hqk,khd->qhd", attn_probs, value_rows, preferred_element_type=jnp.float32
    )
    live_rows = (positions < length)[:, None, None]
    return jnp.where(live_rows, attended, 0.0).astype(jnp.bfloat16)


def contract_rows(lhs, rhs_t):
    return lax.dot_general(lhs, rhs_t, (((1,), (1,)), ((), ())), preferred_element_type=jnp.float32)


def on_device(
    tokens,
    lengths,
    page_slot,
    w_query,
    w_keyval,
    w_out,
    w_gateup,
    w_down,
    attn_gain,
    ffn_gain,
    query_gain,
    key_gain,
):
    col_count = lax.axis_size("col")
    col_index = lax.axis_index("col")
    head_dim = query_gain.shape[0]
    local_width = w_query.shape[1]
    local_heads = local_width // head_dim
    kv_heads = w_keyval.shape[2] // head_dim
    group_size = local_heads * col_count // kv_heads
    assert group_size % local_heads == 0
    kv_head = col_index * local_heads // group_size
    unit_count = w_gateup.shape[2]
    kv_piece = lax.dynamic_slice_in_dim(w_keyval, kv_head * head_dim, head_dim, axis=2)
    pieces = [
        w_query.astype(jnp.bfloat16),
        jnp.transpose(kv_piece.astype(jnp.bfloat16), (1, 0, 2)).reshape(kv_piece.shape[1], -1),
        jnp.transpose(w_out.astype(jnp.bfloat16)),
        jnp.transpose(w_gateup.astype(jnp.bfloat16), (1, 0, 2)).reshape(w_gateup.shape[1], -1),
        jnp.transpose(w_down.astype(jnp.bfloat16)),
    ]
    widths = [p.shape[1] for p in pieces]
    packed = jnp.concatenate(pieces, axis=1)
    full = lax.all_gather(packed, ("row", "page"), axis=0, tiled=True)
    offsets = [sum(widths[:i]) for i in range(len(widths) + 1)]
    qkv_w = full[:, offsets[0] : offsets[2]]
    out_t = full[:, offsets[2] : offsets[3]]
    gateup_w = full[:, offsets[3] : offsets[4]]
    down_t = full[:, offsets[4] : offsets[5]]
    prompt_count, seq_len, local_feat = tokens.shape
    gathered = lax.all_gather(tokens, "col", axis=2, tiled=True)
    model_width = gathered.shape[2]
    attn_in = normalize(gathered.astype(jnp.float32), attn_gain).astype(jnp.bfloat16)
    projected = jnp.dot(attn_in.reshape(-1, model_width), qkv_w, preferred_element_type=jnp.float32)
    projected = projected.reshape(prompt_count, seq_len, local_heads + 2, head_dim)
    queries = rotate(normalize(projected[:, :, :local_heads], query_gain)).astype(jnp.bfloat16)
    keys_one = rotate(normalize(projected[:, :, local_heads : local_heads + 1], key_gain)).astype(
        jnp.bfloat16
    )
    values_one = projected[:, :, local_heads + 1 : local_heads + 2].astype(jnp.bfloat16)
    keys_rot = jnp.broadcast_to(keys_one, queries.shape)
    values_in = jnp.broadcast_to(values_one, queries.shape)
    attended = jnp.stack(
        [
            attend(queries[i], keys_rot[i], values_in[i], lengths[i]).reshape(seq_len, local_width)
            for i in range(prompt_count)
        ]
    )
    attn_terms = contract_rows(attended.reshape(-1, local_width), out_t)
    attn_terms = attn_terms.reshape(prompt_count, seq_len, model_width).astype(jnp.bfloat16)
    attn_sum = lax.psum(attn_terms, "col").astype(jnp.float32)
    residual_all = (gathered.astype(jnp.float32) + attn_sum).astype(jnp.bfloat16)
    residual = lax.dynamic_slice_in_dim(residual_all, col_index * local_feat, local_feat, axis=2)
    ffn_in = normalize(residual_all.astype(jnp.float32), ffn_gain).astype(jnp.bfloat16)
    gate_up = jnp.dot(ffn_in.reshape(-1, model_width), gateup_w, preferred_element_type=jnp.float32)
    hidden = (jax.nn.silu(gate_up[:, :unit_count]) * gate_up[:, unit_count:]).astype(jnp.bfloat16)
    ffn_terms = contract_rows(hidden, down_t).reshape(prompt_count, seq_len, model_width)
    ffn_sum = lax.psum_scatter(
        ffn_terms.astype(jnp.bfloat16), "col", scatter_dimension=2, tiled=True
    ).astype(jnp.float32)
    layer_out = (residual.astype(jnp.float32) + ffn_sum).astype(jnp.bfloat16)
    page_count = lax.axis_size("page")
    page_index = lax.axis_index("page")
    blocks_each = prompt_count * (seq_len // PAGE_LEN)
    capacity = blocks_each // page_count
    owners = page_slot // blocks_each
    local_slot = page_slot % blocks_each
    same_owner = owners[:, :, None] == owners[:, None, :]
    earlier = (
        jnp.arange(blocks_each, dtype=jnp.int32)[None, :]
        < jnp.arange(blocks_each, dtype=jnp.int32)[:, None]
    )
    order_in = jnp.sum((same_owner & earlier[None]).astype(jnp.int32), axis=2)
    my_owners = lax.dynamic_index_in_dim(owners, page_index, 0, keepdims=False)
    my_order = lax.dynamic_index_in_dim(order_in, page_index, 0, keepdims=False)
    send_pos = my_owners * capacity + my_order
    live_rows = (jnp.arange(seq_len, dtype=jnp.int32)[None, :] < lengths[:, None])[:, :, None, None]
    page_keys = jnp.where(live_rows, keys_rot, jnp.zeros_like(keys_rot)).reshape(
        blocks_each, PAGE_LEN, local_width
    )
    page_values = jnp.where(live_rows, values_in, jnp.zeros_like(values_in)).reshape(
        blocks_each, PAGE_LEN, local_width
    )
    stacked = jnp.stack([page_keys, page_values])
    outgoing = jnp.zeros_like(stacked).at[:, send_pos].set(stacked)
    incoming = lax.all_to_all(outgoing, "page", split_axis=1, concat_axis=1, tiled=True)
    arrival_hit = (owners[:, None, :] == page_index) & (
        order_in[:, None, :] == jnp.arange(capacity, dtype=jnp.int32)[None, :, None]
    )
    arrival_slot = jnp.sum(jnp.where(arrival_hit, local_slot[:, None, :], 0), axis=2).reshape(
        blocks_each
    )
    kv_pages = jnp.zeros_like(incoming).at[:, arrival_slot].set(incoming)
    return (layer_out, kv_pages)


def solution(mesh):
    in_specs = (
        P(("row", "page"), None, "col"),
        P(("row", "page")),
        P("row", None),
        P(("row", "page"), "col"),
        P(None, ("row", "page"), None),
        P("col", ("row", "page")),
        P(None, ("row", "page"), "col"),
        P("col", ("row", "page")),
        P(),
        P(),
        P(),
        P(),
    )
    out_specs = (P(("row", "page"), None, "col"), P(None, ("row", "page"), None, "col"))
    return jax.shard_map(
        on_device, mesh=mesh, in_specs=in_specs, out_specs=out_specs, check_vma=False
    )
```

profile of v0, /device:TPU:8, one launch (start us, length us, event | category | flops | bytes accessed | tf_op | source)
XLA Modules:
  0.0 443.9 jit_solution(3106016607968333589)
XLA Ops:
  7.2 0.7 all-gather.3.cloned.1.call-update
  8.3 1.0 convert_bitcast_fusion
  9.3 0.8 convert_dynamic-update-slice_fusion
  10.1 0.8 bitcast_dynamic-update-slice_fusion.1
  10.9 0.9 bitcast_dynamic-update-slice_fusion
  11.8 0.7 copy-done.4
  13.3 1.0 fusion.42
  14.4 74.6 %all-gather.3.cloned.1.call-done = bf16[1,512,2048]{2,1,0:T(8,128)(2,1)} async-done(((bf16[1,512,256]{2,1,0:T(8,128)(2,1)}), bf16[1,512,2048]{2,1,0:T(8,128)(2,1)}) %all-gather.3.cloned.1.call-update) | async-done | bytes 2097168 | tf_op jit(solution)/shard_map/all_gather | solution.py:91
  89.0 2.1 fusion.5
  91.0 91.8 %all-gather.5.cloned.1.call-done = bf16[2048,2304]{1,0:T(8,128)(2,1)} async-done(((bf16[64,2304]{1,0:T(8,128)(2,1)}), bf16[2048,2304]{1,0:T(8,128)(2,1)}) %all-gather.5.cloned.1.call-update) | async-done | bytes 9437200 | tf_op jit(solution)/shard_map/all_gather | solution.py:84
  182.9 1.3 slice_bitcast_fusion
  184.2 1.4 copy.35
  185.6 2.1 fusion.23
  187.9 0.3 fusion.45
  188.5 0.7 fusion.21
  189.2 0.7 fusion.26
  189.9 3.2 fusion.10
  193.2 131.7 %all-reduce.2.cloned.1.call-done = bf16[1,512,2048]{2,1,0:T(8,128)(2,1)} async-done(((bf16[1,512,2048]{2,1,0:T(8,128)(2,1)}), bf16[1,512,2048]{2,1,0:T(8,128)(2,1)}) %all-reduce.2.cloned.1.call-update) | async-done | bytes 2097168 | tf_op jit(solution)/shard_map/psum | solution.py:111
  324.9 2.6 fusion.2
  327.5 6.2 %fusion = f32[512,1280]{1,0:T(8,128)S(1)} fusion(bf16[2048,2304]{1,0:T(8,128)(2,1)} %all-gather.5.cloned.1.call-done, bf16[1,512,2048]{2,1,0:T(8,128)(2,1)S(1)} %get-tuple-element.3, f32[2048]{0:T(1024)S(1)} %copy-done.10, f32[512]{0:T(512)S(1)} %add_rsqrt_fusion.1), kind=kOutput, calls=%fused_computation.7 | convolution fusion | flops 2688548864 | bytes 9971712 | tf_op jit(solution)/shard_map/dot_general | solution.py:115
  333.6 5.0 %fusion.9 = bf16[1,512,2048]{2,1,0:T(8,128)(2,1)} fusion(bf16[2048,2304]{1,0:T(8,128)(2,1)} %all-gather.5.cloned.1.call-done, f32[512,1280]{1,0:T(8,128)S(1)} %fusion), kind=kOutput, calls=%fused_computation.18 | convolution fusion | flops 1345191936 | bytes 7340032 | tf_op jit(solution)/shard_map/dot_general | solution.py:47
  338.7 0.6 copy-done.7
  339.3 0.2 convert_reduce_fusion
  339.8 0.2 maximum_bitcast_fusion
  340.0 0.2 copy.37
  340.3 0.8 scatter_fusion
  341.0 0.7 copy.38
  341.8 5.9 %all-to-all-start = ((bf16[2,4,128,128]{3,2,0,1:T(8,128)(2,1)}), bf16[2,4,128,128]{3,2,0,1:T(8,128)(2,1)S(1)}, u32[]{:S(2)}, u32[]{:S(2)}) async-start(bf16[2,4,128,128]{3,2,0,1:T(8,128)(2,1)} %copy.38), calls=%async_computation.1 | async-start | bytes 524288 | tf_op jit(solution)/shard_map/all_to_all | solution.py:146
  347.8 6.7 %all-to-all-done = bf16[2,4,128,128]{3,2,0,1:T(8,128)(2,1)S(1)} async-done(((bf16[2,4,128,128]{3,2,0,1:T(8,128)(2,1)}), bf16[2,4,128,128]{3,2,0,1:T(8,128)(2,1)S(1)}, u32[]{:S(2)}, u32[]{:S(2)}) %all-to-all-start) | async-done | bytes 262176 | tf_op jit(solution)/shard_map/all_to_all | solution.py:146
  354.6 0.8 scatter_fusion.1
  355.4 80.2 %reduce-scatter.2.cloned.1.call-done = bf16[1,512,256]{2,1,0:T(8,128)(2,1)} async-done(((bf16[1,512,2048]{2,1,0:T(8,128)(2,1)}), bf16[1,512,256]{2,1,0:T(8,128)(2,1)}) %reduce-scatter.2.cloned.1.call-update) | async-done | bytes 262160 | tf_op jit(solution)/shard_map/reduce_scatter | solution.py:118
  435.6 1.8 add_convert_fusion
  (60 shorter events, 1.5 us)
Async XLA Ops:
  7.2 0.9 copy-start
  7.2 81.8 %all-gather.3.cloned.1.call-start = ((), (), s32[]{:S(2)}) async-start(), calls=%async_computation.2 | async-start | bytes 2359296 | tf_op jit(solution)/shard_map/all_gather | solution.py:91
  7.9 174.9 %all-gather.5.cloned.1.call-start = ((), (), s32[]{:S(2)}) async-start(), calls=%async_computation.3 | async-start | bytes 9732096 | tf_op jit(solution)/shard_map/all_gather | solution.py:84
  11.8 0.7 copy-start.4
  12.5 312.3 %all-reduce.2.cloned.1.call-start = ((), (), s32[]{:S(2)}) async-start(), calls=%async_computation.4 | async-start | bytes 4194304 | tf_op jit(solution)/shard_map/psum | solution.py:111
  91.0 94.6 %copy-start.1 = (bf16[1,512,2048]{2,1,0:T(8,128)(2,1)S(1)}, bf16[1,512,2048]{2,1,0:T(8,128)(2,1)}, u32[]{:S(2)}) copy-start(bf16[1,512,2048]{2,1,0:T(8,128)(2,1)} %all-gather.3.cloned.1.call-done) | copy-start | bytes 6291460
  185.6 2.2 copy-start.8
  185.6 2.7 copy-start.9
  185.6 2.8 copy-start.5
  185.6 2.8 copy-start.6
  193.1 134.3 %copy-start.10 = (f32[2048]{0:T(1024)S(1)}, f32[2048]{0:T(1024)}, u32[]{:S(2)}) copy-start(f32[2048]{0:T(1024)} %param.21) | copy-start | bytes 24580
  193.2 242.5 %reduce-scatter.2.cloned.1.call-start = ((), (), s32[]{:S(2)}) async-start(), calls=%async_computation.5 | async-start | bytes 2359296 | tf_op jit(solution)/shard_map/reduce_scatter | solution.py:118
  327.4 6.2 %copy-start.2 = (bf16[1,512,2048]{2,1,0:T(8,128)(2,1)}, bf16[1,512,2048]{2,1,0:T(8,128)(2,1)S(1)}, u32[]{:S(2)}) copy-start(bf16[1,512,2048]{2,1,0:T(8,128)(2,1)S(1)} %get-tuple-element.3) | copy-start | bytes 6291460
  338.7 0.7 copy-start.7
  341.8 12.8 %all-to-all-start = ((bf16[2,4,128,128]{3,2,0,1:T(8,128)(2,1)}), bf16[2,4,128,128]{3,2,0,1:T(8,128)(2,1)S(1)}, u32[]{:S(2)}, u32[]{:S(2)}) async-start(bf16[2,4,128,128]{3,2,0,1:T(8,128)(2,1)} %copy.38), calls=%async_computation.1 | async-start | bytes 524288 | tf_op jit(solution)/shard_map/all_to_all | solution.py:146
  355.4 82.0 %copy-start.3 = (bf16[2,4,128,128]{3,2,1,0:T(8,128)(2,1)}, bf16[2,4,128,128]{3,2,1,0:T(8,128)(2,1)S(1)}, u32[]{:S(2)}) copy-start(bf16[2,4,128,128]{3,2,1,0:T(8,128)(2,1)S(1)} %scatter_fusion.1) | copy-start | bytes 786436
Sparse Core Ops, SparseCore 0:
  10.5 78.4 all-gather.2
  90.8 92.0 all-gather.4
  193.3 131.5 all-reduce.1
  338.8 96.7 reduce-scatter.1
where the time goes:
time: 445 us; the launch traced here: 444 us
  waiting for transfers between devices  386 us (87%)
  matrix products  17.9 us (4%)
  between operations  14.8 us (3%)
  other arithmetic  12.3 us (3%)
  local copies, waits for them, and re-layouts  7.11 us (2%)
  starting transfers between devices  6.08 us (1%)
    psum x1, waiting for transfers between devices, on_device(): attn_sum = lax.psum(attn_terms, 'col').astype(jnp.float32)  132 us
    all_gather x1, waiting for transfers between devices, on_device(): full = lax.all_gather(packed, ('row', 'page'), axis=0, tiled=True)  91.8 us
    reduce_scatter x1, waiting for transfers between devices, on_device(): lax.psum_scatter(ffn_terms.astype(jnp.bfloat16), 'col', scatter_dimension...  80.2 us
    all_gather x1, waiting for transfers between devices, on_device(): gathered = lax.all_gather(tokens, 'col', axis=2, tiled=True)  74.6 us
  transfers between devices with their start and end apart: 5, of which 5 were waited for; matrix products, arithmetic and copies ran while one was open for 2% of the time, Pallas kernels for 0%

commit v1 on v0

--- a/solution.py
+++ b/solution.py
@@ -2,8 +2,22 @@
 import jax.numpy as jnp
 from jax import lax
 from jax.sharding import PartitionSpec as P
+from jax.lax import all_to_all, axis_size
 
 PAGE_LEN = 128
+
+
+def pack_yards(matrix, axis_k):
+    carry_in = jnp.concatenate(
+        all_to_all(
+            jnp.stack([matrix] * axis_size(("row", "page")), axis=0),
+            axis_name=("row", "page"),
+            split_axis=0,
+            concat_axis=0,
+        ),
+        axis_k,
+    )
+    return carry_in
 
 
 def normalize(values, norm_gain):
@@ -81,7 +95,7 @@
     ]
     widths = [p.shape[1] for p in pieces]
     packed = jnp.concatenate(pieces, axis=1)
-    full = lax.all_gather(packed, ("row", "page"), axis=0, tiled=True)
+    full = pack_yards(packed, 0)
     offsets = [sum(widths[:i]) for i in range(len(widths) + 1)]
     qkv_w = full[:, offsets[0] : offsets[2]]
     out_t = full[:, offsets[2] : offsets[3]]

time: 445 us -> 520 us (1.17)
  waiting for transfers between devices: 386 us -> 447 us
  starting transfers between devices: 6.08 us -> 15.2 us
    all_to_all x0 -> x1, waiting for transfers between devices: none -> 130 us  [pack_yards(): all_to_all(jnp.stack([matrix] * axis_size(('row', 'page')), axis=0), axis...]
    all_gather x1 -> x0, waiting for transfers between devices: 91.8 us -> none  [on_device(): full = lax.all_gather(packed, ('row', 'page'), axis=0, tiled=True)]
    all_gather x1, waiting for transfers between devices: 74.6 us -> 92.7 us  [on_device(): gathered = lax.all_gather(tokens, 'col', axis=2, tiled=True)]
    all_to_all x0 -> x1, starting transfers between devices: none -> 9.18 us  [pack_yards(): all_to_all(jnp.stack([matrix] * axis_size(('row', 'page')), axis=0), axis...]
  transfers between devices with their start and end apart: 5 -> 5, of which waited for: 5 -> 5; matrix products, arithmetic and copies ran while one was open for 2% -> 1% of each run, Pallas kernels for 0% -> 0%
where the time goes in v1:
time: 520 us; the launch traced here: 519 us
  waiting for transfers between devices  447 us (86%)
  matrix products  17.9 us (3%)
  starting transfers between devices  15.2 us (3%)
  between operations  14.7 us (3%)
  other arithmetic  12.3 us (2%)
  local copies, waits for them, and re-layouts  12 us (2%)
    psum x1, waiting for transfers between devices, on_device(): attn_sum = lax.psum(attn_terms, 'col').astype(jnp.float32)  137 us
    all_to_all x1, waiting for transfers between devices, pack_yards(): all_to_all(jnp.stack([matrix] * axis_size(('row', 'page')), axis=0), axis...  130 us
    all_gather x1, waiting for transfers between devices, on_device(): gathered = lax.all_gather(tokens, 'col', axis=2, tiled=True)  92.7 us
    reduce_scatter x1, waiting for transfers between devices, on_device(): lax.psum_scatter(ffn_terms.astype(jnp.bfloat16), 'col', scatter_dimension...  80.5 us
  transfers between devices with their start and end apart: 5, of which 5 were waited for; matrix products, arithmetic and copies ran while one was open for 1% of the time, Pallas kernels for 0%

profile of v1, /device:TPU:8, one launch (start us, length us, event | category | flops | bytes accessed | tf_op | source)
XLA Modules:
  0.0 519.1 jit_solution(15339647319856996533)
XLA Ops:
  7.2 0.9 copy-done
  8.3 0.8 convert_dynamic-update-slice_fusion
  9.1 1.0 convert_bitcast_fusion
  10.1 0.8 bitcast_dynamic-update-slice_fusion.1
  10.9 0.9 bitcast_dynamic-update-slice_fusion
  11.8 4.7 stack.4
  16.5 9.2 %all-to-all-start = ((bf16[32,64,2304]{2,1,0:T(8,128)(2,1)}), bf16[32,64,2304]{2,1,0:T(8,128)(2,1)}, u32[]{:S(2)}, u32[]{:S(2)}) async-start(bf16[32,64,2304]{2,1,0:T(8,128)(2,1)} %stack.4), calls=%async_computation | async-start | bytes 18874368 | tf_op jit(solution)/shard_map/all_to_all | solution.py:12
  25.8 0.7 all-gather.2.cloned.1.call-update
  27.2 1.0 fusion.42
  28.3 92.7 %all-gather.2.cloned.1.call-done = bf16[1,512,2048]{2,1,0:T(8,128)(2,1)} async-done(((bf16[1,512,256]{2,1,0:T(8,128)(2,1)}), bf16[1,512,2048]{2,1,0:T(8,128)(2,1)}) %all-gather.2.cloned.1.call-update) | async-done | bytes 2097168 | tf_op jit(solution)/shard_map/all_gather | solution.py:105
  121.0 2.1 fusion.5
  123.0 129.6 %all-to-all-done = bf16[32,64,2304]{2,1,0:T(8,128)(2,1)} async-done(((bf16[32,64,2304]{2,1,0:T(8,128)(2,1)}), bf16[32,64,2304]{2,1,0:T(8,128)(2,1)}, u32[]{:S(2)}, u32[]{:S(2)}) %all-to-all-start) | async-done | bytes 9437216 | tf_op jit(solution)/shard_map/all_to_all | solution.py:12
  252.7 1.4 slice_bitcast_fusion
  254.1 1.4 copy.35
  255.6 2.1 fusion.23
  257.9 0.3 fusion.45
  258.4 0.7 fusion.21
  259.2 0.7 fusion.26
  259.9 3.2 fusion.10
  263.2 136.6 %all-reduce.2.cloned.1.call-done = bf16[1,512,2048]{2,1,0:T(8,128)(2,1)} async-done(((bf16[1,512,2048]{2,1,0:T(8,128)(2,1)}), bf16[1,512,2048]{2,1,0:T(8,128)(2,1)}) %all-reduce.2.cloned.1.call-update) | async-done | bytes 2097168 | tf_op jit(solution)/shard_map/psum | solution.py:125
  399.8 2.6 fusion.2
  402.4 6.2 %fusion = f32[512,1280]{1,0:T(8,128)S(1)} fusion(bf16[2048,2304]{1,0:T(8,128)(2,1)} %bitcast.7, bf16[1,512,2048]{2,1,0:T(8,128)(2,1)S(1)} %get-tuple-element.3, f32[2048]{0:T(1024)S(1)} %copy-done.9, f32[512]{0:T(512)S(1)} %add_rsqrt_fusion.1), kind=kOutput, calls=%fused_computation.7 | convolution fusion | flops 2688548864 | bytes 9971712 | tf_op jit(solution)/shard_map/dot_general | solution.py:129
  408.5 5.0 fusion.9
  413.6 0.6 copy-done.6
  414.2 0.2 convert_reduce_fusion
  415.2 0.8 scatter_fusion
  415.9 0.7 copy.38
  416.7 5.9 %all-to-all-start.1 = ((bf16[2,4,128,128]{3,2,0,1:T(8,128)(2,1)}), bf16[2,4,128,128]{3,2,0,1:T(8,128)(2,1)S(1)}, u32[]{:S(2)}, u32[]{:S(2)}) async-start(bf16[2,4,128,128]{3,2,0,1:T(8,128)(2,1)} %copy.38), calls=%async_computation.2 | async-start | bytes 524288 | tf_op jit(solution)/shard_map/all_to_all | solution.py:160
  422.7 6.7 %all-to-all-done.1 = bf16[2,4,128,128]{3,2,0,1:T(8,128)(2,1)S(1)} async-done(((bf16[2,4,128,128]{3,2,0,1:T(8,128)(2,1)}), bf16[2,4,128,128]{3,2,0,1:T(8,128)(2,1)S(1)}, u32[]{:S(2)}, u32[]{:S(2)}) %all-to-all-start.1) | async-done | bytes 262176 | tf_op jit(solution)/shard_map/all_to_all | solution.py:160
  429.5 0.8 scatter_fusion.1
  430.3 80.5 %reduce-scatter.2.cloned.1.call-done = bf16[1,512,256]{2,1,0:T(8,128)(2,1)} async-done(((bf16[1,512,2048]{2,1,0:T(8,128)(2,1)}), bf16[1,512,256]{2,1,0:T(8,128)(2,1)}) %reduce-scatter.2.cloned.1.call-update) | async-done | bytes 262160 | tf_op jit(solution)/shard_map/reduce_scatter | solution.py:132
  510.8 1.8 add_convert_fusion
  (58 shorter events, 1.8 us)
Async XLA Ops:
  7.2 0.9 copy-start
  16.5 236.1 %all-to-all-start = ((bf16[32,64,2304]{2,1,0:T(8,128)(2,1)}), bf16[32,64,2304]{2,1,0:T(8,128)(2,1)}, u32[]{:S(2)}, u32[]{:S(2)}) async-start(bf16[32,64,2304]{2,1,0:T(8,128)(2,1)} %stack.4), calls=%async_computation | async-start | bytes 18874368 | tf_op jit(solution)/shard_map/all_to_all | solution.py:12
  25.7 95.2 %all-gather.2.cloned.1.call-start = ((), (), s32[]{:S(2)}) async-start(), calls=%async_computation.3 | async-start | bytes 2359296 | tf_op jit(solution)/shard_map/all_gather | solution.py:105
  26.5 373.3 %all-reduce.2.cloned.1.call-start = ((), (), s32[]{:S(2)}) async-start(), calls=%async_computation.4 | async-start | bytes 4194304 | tf_op jit(solution)/shard_map/psum | solution.py:125
  252.7 2.9 copy-start.1
  255.5 2.3 copy-start.7
  255.6 2.7 copy-start.8
  255.6 2.8 copy-start.4
  255.6 2.8 copy-start.5
  263.1 139.3 %copy-start.9 = (f32[2048]{0:T(1024)S(1)}, f32[2048]{0:T(1024)}, u32[]{:S(2)}) copy-start(f32[2048]{0:T(1024)} %param.21) | copy-start | bytes 24580
  263.1 247.7 %reduce-scatter.2.cloned.1.call-start = ((), (), s32[]{:S(2)}) async-start(), calls=%async_computation.5 | async-start | bytes 2359296 | tf_op jit(solution)/shard_map/reduce_scatter | solution.py:132
  402.3 6.2 %copy-start.2 = (bf16[1,512,2048]{2,1,0:T(8,128)(2,1)}, bf16[1,512,2048]{2,1,0:T(8,128)(2,1)S(1)}, u32[]{:S(2)}) copy-start(bf16[1,512,2048]{2,1,0:T(8,128)(2,1)S(1)} %get-tuple-element.3) | copy-start | bytes 6291460
  413.6 0.7 copy-start.6
  416.7 12.8 %all-to-all-start.1 = ((bf16[2,4,128,128]{3,2,0,1:T(8,128)(2,1)}), bf16[2,4,128,128]{3,2,0,1:T(8,128)(2,1)S(1)}, u32[]{:S(2)}, u32[]{:S(2)}) async-start(bf16[2,4,128,128]{3,2,0,1:T(8,128)(2,1)} %copy.38), calls=%async_computation.2 | async-start | bytes 524288 | tf_op jit(solution)/shard_map/all_to_all | solution.py:160
  430.3 82.3 %copy-start.3 = (bf16[2,4,128,128]{3,2,1,0:T(8,128)(2,1)}, bf16[2,4,128,128]{3,2,1,0:T(8,128)(2,1)S(1)}, u32[]{:S(2)}) copy-start(bf16[2,4,128,128]{3,2,1,0:T(8,128)(2,1)S(1)} %scatter_fusion.1) | copy-start | bytes 786436
Sparse Core Ops, SparseCore 0:
  29.0 91.9 all-gather.1
  263.2 136.4 all-reduce.1
  413.7 97.0 reduce-scatter.1
